TPU v7x, 256 devices: a whole 4x4x8 slice. The times are simulated.
256 devices in a mesh: batch: 8 (over x, core), tensor: 32 (over y, z).
Axes of the slice: x: 4, y: 4, z: 8, core: 2. Of those that a mesh axis runs over, the one named last changes fastest.
Arguments:
- inputs: bfloat16 [4, 8, 32, 4096], P(None, 'batch', 'tensor'), may hold values from -6 to 6
- norm_gain: float32 [4096], replicated, may hold values from 0.5 to 1.5
- norm_bias: float32 [4096], replicated, may hold values from -3 to 3
- qkv_weight: bfloat16 [4096, 3, 4096], P(None, None, 'tensor'), may hold values from -0.09375 to 0.09375
- out_weight: bfloat16 [4096, 4096], P('tensor'), may hold values from -0.375 to 0.375
- in_weight: bfloat16 [4096, 8192], P(None, 'tensor'), may hold values from -0.09375 to 0.09375
- in_bias: float32 [8192], P('tensor'), may hold values from -3 to 3
- down_weight: bfloat16 [8192, 4096], P('tensor'), may hold values from -0.0625 to 0.0625
- down_bias: float32 [4096], replicated, may hold values from -3 to 3
- page_pool: bfloat16 [128, 2, 128, 4096], P('batch', None, None, 'tensor'), may hold values from -103 to 103
- old_cache: bfloat16 [8, 32, 2, 64, 4096], P('batch', None, None, None, 'tensor'), may hold values from -103 to 103, as said below
- page_table: int32 [32, 4], replicated, may hold values from 0 to 127, as said below
- prompt_length: int32 [32], replicated, may hold values from 1 to 512, 8192 in all
- parents: int32 [4, 8, 32], replicated, may hold values from 0 to 7
Outputs:
- outputs: float32 [4, 8, 32, 4096], P(None, 'batch', 'tensor')
Inputs may be any that keep to these rules, and one draw needn't show every extreme that they name: `old_cache`: key and value entries of the beams' generated tokens. `page_table`: every pool page is named exactly once in the table. The pool is cut into as many equal blocks of consecutive pages as the batch axis has devices; request r names only pages of block r modulo that count.
All inputs are finite; a program needn't handle non-finite values.
Results may differ from a plain program's by a relative error of at most 0.034.
Values may be sent and summed in bfloat16 or wider, within the bound.
No kernel may reach another device: no remote copies, remote signals or barrier semaphores. Data moves between devices by JAX's collectives and lax.ppermute only.
A program may use at most 128 MiB of HBM per device.

v0:
```python
import math
import jax
import jax.numpy as jnp
from jax import lax
from jax.sharding import PartitionSpec as P

HDIM = 256
ROT = 64
BEAMS = 8
STEPS = 4
NEG_FILL = -1e30


def partner(value, axis, bit):
    return lax.ppermute(value, axis, [(i, i ^ 1 << bit) for i in range(lax.axis_size(axis))])


def joined_2(part, axis, combine):
    gathered = jax.tree.map(lambda a: lax.all_gather(a, axis), part)

    def take(source):
        return jax.tree.map(lambda a: lax.dynamic_index_in_dim(a, source, 0, False), gathered)

    return lax.fori_loop(
        1, lax.axis_size(axis), lambda source, state: combine(state, take(source)), take(0)
    )


def normalize(row_block, norm_gain, norm_bias):
    widened = row_block.astype(jnp.float32)
    center = jnp.mean(widened, axis=-1, keepdims=True)
    shifted = widened - center
    variance = jnp.mean(shifted * shifted, axis=-1, keepdims=True)
    return shifted * lax.rsqrt(variance + 1e-05) * norm_gain + norm_bias


def rotate_local(vectors, position, first_column):
    half_count = vectors.shape[-1] // 2
    doubled = (first_column + 2 * jnp.arange(half_count)) % HDIM
    exponent = doubled.astype(jnp.float32) / ROT
    frequency = jnp.where(doubled < ROT, jnp.exp(-exponent * math.log(10000.0)), 0.0)
    angles = position[:, None] * frequency[None, :]
    cosine = jnp.cos(angles)[None]
    sine_part = jnp.sin(angles)[None]
    halves = vectors.reshape(vectors.shape[:-1] + (half_count, 2))
    even_part = halves[..., 0]
    odd_part = halves[..., 1]
    turned = jnp.stack(
        [even_part * cosine - odd_part * sine_part, odd_part * cosine + even_part * sine_part],
        axis=-1,
    )
    return turned.reshape(vectors.shape)


def combine(earlier, later):
    peak_one, total_one, mixture_one = earlier
    peak_two, total_two, mixture_two = later
    peak = jnp.maximum(peak_one, peak_two)
    factor_one = jnp.exp(peak_one - peak)
    factor_two = jnp.exp(peak_two - peak)
    return (
        peak,
        total_one * factor_one + total_two * factor_two,
        mixture_one * factor_one[..., None] + mixture_two * factor_two[..., None],
    )


def partial_softmax(scores, allowed):
    masked = jnp.where(allowed, scores, NEG_FILL)
    peak = jnp.max(masked, axis=-1)
    weights = jnp.where(allowed, jnp.exp(masked - peak[..., None]), 0.0)
    return (peak, jnp.sum(weights, axis=-1), weights.astype(jnp.bfloat16))


def place_block(values, slot, slot_count, axis, fill_value):
    hit_shape = [1] * (values.ndim + 1)
    hit_shape[axis] = slot_count
    hits = (jnp.arange(slot_count) == slot).reshape(hit_shape)
    return jnp.where(hits, jnp.expand_dims(values, axis), fill_value)


def head_sum(prompt_scores, chain_scores):
    other_prompt, other_chain = partner((prompt_scores, chain_scores), "tensor", 0)
    prompt_scores = prompt_scores + other_prompt
    chain_scores = chain_scores + other_chain
    return (prompt_scores, chain_scores)


def on_device(
    inputs,
    norm_gain,
    norm_bias,
    qkv_weight,
    out_weight,
    in_weight,
    in_bias,
    down_weight,
    down_bias,
    page_pool,
    old_cache,
    page_table,
    prompt_length,
    parents,
):
    batch_index = lax.axis_index("batch")
    tensor_index = lax.axis_index("tensor")
    groups = lax.axis_size("batch")
    beam_dev = inputs.shape[1]
    model_width = inputs.shape[3]
    columns = qkv_weight.shape[2]
    requests = page_table.shape[0]
    history = old_cache.shape[3]
    prompt_span = page_table.shape[1] * page_pool.shape[2]
    heads_dev = max(columns // HDIM, 1)
    head_part = min(columns, HDIM)
    scale_factor = HDIM ** (-0.5)
    qkv_flat = qkv_weight.reshape(model_width, 3 * columns)
    first_column = tensor_index * columns
    owners = batch_index * beam_dev + jnp.arange(beam_dev)
    old_keys = old_cache[:, :, 0].reshape(beam_dev, requests, history, heads_dev, head_part)
    old_values = old_cache[:, :, 1].reshape(beam_dev, requests, history, heads_dev, head_part)
    stored_keys = jnp.zeros((beam_dev, requests, STEPS, columns), jnp.bfloat16)
    stored_values = jnp.zeros((beam_dev, requests, STEPS, columns), jnp.bfloat16)
    beam_ids = jnp.broadcast_to(jnp.arange(BEAMS)[:, None], (BEAMS, requests))
    prompt_ok = jnp.arange(prompt_span)[None, :] < prompt_length[:, None]
    whole_pool = lax.all_gather(page_pool, "batch", axis=0, tiled=True)
    page_rows = whole_pool[page_table]
    count_rows = page_table.shape[0]
    prompt_keys = page_rows[:, :, 0].reshape(count_rows, prompt_span, heads_dev, head_part)
    prompt_values = page_rows[:, :, 1].reshape(count_rows, prompt_span, heads_dev, head_part)
    outputs = []
    for step_index in range(STEPS):
        current = inputs[step_index]
        normed = normalize(current, norm_gain, norm_bias).astype(jnp.bfloat16)
        gathered_rows = lax.all_gather(normed, "tensor", axis=1, tiled=True)
        attn_part = jnp.einsum(
            "brd,dc->brc", gathered_rows, qkv_flat, preferred_element_type=jnp.float32
        )
        ffn_part = jnp.einsum(
            "brd,dc->brc", gathered_rows, in_weight, preferred_element_type=jnp.float32
        )
        projected = jnp.concatenate([attn_part, ffn_part], axis=-1)
        position = (prompt_length + history + step_index).astype(jnp.float32)
        queries = rotate_local(projected[..., :columns], position, first_column).astype(
            jnp.bfloat16
        )
        fresh_keys = rotate_local(
            projected[..., columns : 2 * columns], position, first_column
        ).astype(jnp.bfloat16)
        fresh_values = projected[..., 2 * columns : 3 * columns].astype(jnp.bfloat16)
        hidden = jax.nn.gelu(projected[..., 3 * columns :] + in_bias, approximate=True).astype(
            jnp.bfloat16
        )
        stored_keys = stored_keys.at[:, :, step_index].set(fresh_keys)
        stored_values = stored_values.at[:, :, step_index].set(fresh_values)
        queries_all = lax.all_gather(queries, "batch", axis=0, tiled=True)
        query_heads = queries_all.reshape(BEAMS, requests, heads_dev, head_part)
        own_heads = queries.reshape(beam_dev, requests, heads_dev, head_part)
        ancestry = []
        lineage = beam_ids
        for back_step in range(step_index, -1, -1):
            ancestry.append(lineage)
            lineage = jnp.take_along_axis(parents[back_step], lineage, axis=0)
        unused_steps = [jnp.full_like(beam_ids, -1)] * (STEPS - 1 - step_index)
        ancestry_all = jnp.stack(ancestry[::-1] + unused_steps, axis=-1)
        stored_k = stored_keys.reshape(beam_dev, requests, STEPS, heads_dev, head_part)
        stored_v = stored_values.reshape(beam_dev, requests, STEPS, heads_dev, head_part)
        chain_scores = (
            jnp.concatenate(
                [
                    jnp.einsum(
                        "brnd,jrtnd->brnjt",
                        query_heads,
                        old_keys,
                        preferred_element_type=jnp.float32,
                    ),
                    jnp.einsum(
                        "brnd,jrtnd->brnjt",
                        query_heads,
                        stored_k,
                        preferred_element_type=jnp.float32,
                    ),
                ],
                axis=-1,
            )
            * scale_factor
        )
        old_ok = jnp.broadcast_to(
            (lineage[:, :, None] == owners[None, None, :])[:, :, :, None],
            (BEAMS, requests, beam_dev, history),
        )
        new_ok = ancestry_all[:, :, None, :] == owners[None, None, :, None]
        chain_ok = jnp.concatenate([old_ok, new_ok], axis=-1)
        prompt_scores = (
            jnp.einsum(
                "brnd,rtnd->brnt", own_heads, prompt_keys, preferred_element_type=jnp.float32
            )
            * scale_factor
        )
        prompt_scores, chain_scores = head_sum(prompt_scores, chain_scores)
        prompt_peak, prompt_total, prompt_weights = partial_softmax(
            prompt_scores, prompt_ok[None, :, None, :]
        )
        prompt_mix = jnp.einsum(
            "brnt,rtnd->brnd", prompt_weights, prompt_values, preferred_element_type=jnp.float32
        )
        peak_full = place_block(prompt_peak, batch_index, groups, 0, NEG_FILL).reshape(
            BEAMS, requests, heads_dev
        )
        total_full = place_block(prompt_total, batch_index, groups, 0, 0.0).reshape(
            BEAMS, requests, heads_dev
        )
        mix_full = place_block(prompt_mix, batch_index, groups, 0, 0.0).reshape(
            BEAMS, requests, heads_dev, head_part
        )
        chain_peak, chain_total, chain_weights = partial_softmax(
            chain_scores.reshape(BEAMS, requests, heads_dev, -1), chain_ok
        )
        chain_weights = chain_weights.reshape(BEAMS, requests, heads_dev, beam_dev, history + STEPS)
        chain_mix = jnp.einsum(
            "brnjt,jrtnd->brnd",
            chain_weights[..., :history],
            old_values,
            preferred_element_type=jnp.float32,
        )
        chain_mix = chain_mix + jnp.einsum(
            "brnjt,jrtnd->brnd",
            chain_weights[..., history:],
            stored_v,
            preferred_element_type=jnp.float32,
        )
        joined = combine((peak_full, total_full, mix_full), (chain_peak, chain_total, chain_mix))
        merged = joined_2((joined[0], joined[1], joined[2]), "batch", combine)
        first_beam = batch_index * beam_dev
        total_own = lax.dynamic_slice_in_dim(merged[1], first_beam, beam_dev, 0)
        mix_own = lax.dynamic_slice_in_dim(merged[2], first_beam, beam_dev, 0)
        attention = (
            (mix_own / total_own[..., None])
            .reshape(beam_dev, requests, columns)
            .astype(jnp.bfloat16)
        )
        summed = lax.psum_scatter(
            jnp.einsum("brc,cd->rbd", attention, out_weight, preferred_element_type=jnp.float32)
            + jnp.einsum("brf,fd->rbd", hidden, down_weight, preferred_element_type=jnp.float32),
            "tensor",
            scatter_dimension=0,
            tiled=True,
        )
        update = jnp.transpose(summed, (1, 0, 2))
        result = current.astype(jnp.float32) + update + down_bias
        outputs.append(result)
    return jnp.stack(outputs, axis=0)


def solution(mesh):
    in_specs = (
        P(None, "batch", "tensor", None),
        P(),
        P(),
        P(None, None, "tensor"),
        P("tensor", None),
        P(None, "tensor"),
        P("tensor"),
        P("tensor", None),
        P(),
        P("batch", None, None, "tensor"),
        P("batch", None, None, None, "tensor"),
        P(),
        P(),
        P(),
    )
    out_specs = P(None, "batch", "tensor", None)
    return jax.shard_map(
        on_device, mesh=mesh, in_specs=in_specs, out_specs=out_specs, check_vma=False
    )
```

profile of v0, /device:TPU:2, one launch (start us, length us, event | category | flops | bytes accessed | tf_op | source)
XLA Modules:
  0.0 820.2 jit_solution(18254087234877689215)
XLA Ops:
  7.3 1.7 convert_reduce_fusion.1
  11.6 1.7 fusion.214
  17.8 52.7 %all-gather.4 = bf16[131072]{0:T(1024)(128)(2,1)S(1)} all-gather(bf16[4096]{0:T(1024)(128)(2,1)S(1)} %get-tuple-element.1398), channel_id=6, replica_groups=mesh['batch'=8,'tensor'=32] {'tensor'}, dimensions={0}, use_global_device_ids=true | all-gather | bytes 270336 | tf_op jit(solution)/shard_map/all_gather | solution.py:135
  70.6 48.3 %all-gather.2 = bf16[131072]{0:T(1024)(128)(2,1)S(1)} all-gather(bf16[4096]{0:T(1024)(128)(2,1)S(1)} %get-tuple-element.1399), channel_id=4, replica_groups=mesh['batch'=8,'tensor'=32] {'tensor'}, dimensions={0}, use_global_device_ids=true | all-gather | bytes 270336 | tf_op jit(solution)/shard_map/all_gather | solution.py:135
  119.0 47.0 %all-gather = bf16[131072]{0:T(1024)(128)(2,1)S(1)} all-gather(bf16[4096]{0:T(1024)(128)(2,1)S(1)} %get-tuple-element.1400), channel_id=2, replica_groups=mesh['batch'=8,'tensor'=32] {'tensor'}, dimensions={0}, use_global_device_ids=true | all-gather | bytes 270336 | tf_op jit(solution)/shard_map/all_gather | solution.py:135
  166.8 48.2 %all-gather.6 = bf16[131072]{0:T(1024)(128)(2,1)S(1)} all-gather(bf16[4096]{0:T(1024)(128)(2,1)S(1)} %get-tuple-element.1401), channel_id=8, replica_groups=mesh['batch'=8,'tensor'=32] {'tensor'}, dimensions={0}, use_global_device_ids=true | all-gather | bytes 270336 | tf_op jit(solution)/shard_map/all_gather | solution.py:135
  215.2 4.8 copy.1379
  220.0 2.9 convolution_bitcast_fusion.12
  224.5 2.9 convolution_bitcast_fusion.13
  229.5 2.9 convolution_bitcast_fusion.14
  234.6 3.1 convolution_bitcast_fusion.15
  245.7 1.6 fusion.292
  249.0 1.5 copy.1445
  250.4 1.6 fusion.293
  256.3 1.6 fusion.294
  260.8 1.4 copy.1390
  262.2 1.6 fusion.295
  266.7 1.7 fusion.175
  278.8 12.8 %all_gather.91 = bf16[8,32,128]{2,1,0:T(8,128)(2,1)S(1)} all-gather(bf16[1,32,128]{2,1,0:T(8,128)(2,1)S(1)} %copy.1416), channel_id=1, replica_groups=mesh['batch'=8,'tensor'=32] {'batch'}, dimensions={0}, use_global_device_ids=true | all-gather | bytes 73728 | tf_op jit(solution)/shard_map/all_gather | solution.py:156
  293.2 13.0 %all_gather.97 = bf16[8,32,128]{2,1,0:T(8,128)(2,1)S(1)} all-gather(bf16[1,32,128]{2,1,0:T(8,128)(2,1)} %copy.1443), channel_id=1, replica_groups=mesh['batch'=8,'tensor'=32] {'batch'}, dimensions={0}, use_global_device_ids=true | all-gather | bytes 73728 | tf_op jit(solution)/shard_map/all_gather | solution.py:156
  307.7 13.1 %all_gather.103 = bf16[8,32,128]{2,1,0:T(8,128)(2,1)S(1)} all-gather(bf16[1,32,128]{2,1,0:T(8,128)(2,1)} %copy.1470), channel_id=1, replica_groups=mesh['batch'=8,'tensor'=32] {'batch'}, dimensions={0}, use_global_device_ids=true | all-gather | bytes 73728 | tf_op jit(solution)/shard_map/all_gather | solution.py:156
  323.8 1.7 maximum_multiply_fusion.2
  325.5 2.0 collective-permute-start.5
  329.5 12.8 %all_gather.85 = bf16[8,32,128]{2,1,0:T(8,128)(2,1)S(1)} all-gather(bf16[1,32,128]{2,1,0:T(8,128)(2,1)S(1)} %copy.1387), channel_id=1, replica_groups=mesh['batch'=8,'tensor'=32] {'batch'}, dimensions={0}, use_global_device_ids=true | all-gather | bytes 73728 | tf_op jit(solution)/shard_map/all_gather | solution.py:156
  343.6 2.0 collective-permute-start.1
  371.9 1.5 copy.1385
  374.7 1.5 copy.1468
  396.3 10.0 %gather_fusion = bf16[128,2,128,128]{3,2,1,0:T(8,128)(2,1)} fusion(bf16[128,2,128,128]{3,2,1,0:T(8,128)(2,1)} %all-gather.14.cloned.1.call-done, s32[1024]{0:T(1024)S(1)} %pad_clamp_fusion), kind=kCustom, calls=%fused_computation.10 | custom fusion | bytes 16777728 | tf_op jit(solution)/shard_map/gather | solution.py:127
  406.3 4.0 fusion.287
  415.6 2.0 collective-permute-start.4
  417.7 1.9 collective-permute-start
  428.0 3.8 fusion.107
  431.8 3.8 fusion.80
  437.9 2.8 fusion.52
  446.8 2.8 fusion.48
  449.7 1.5 fusion.19
  451.2 3.8 fusion.89
  455.0 3.7 fusion.98
  465.0 12.9 %all_gather.87 = f32[8,8,32,1]{2,1,3,0:T(8,128)S(1)} all-gather(f32[1,8,32,1]{2,1,3,0:T(8,128)S(1)} %get-tuple-element.1418), channel_id=1, replica_groups=mesh['batch'=8,'tensor'=32] {'batch'}, dimensions={0}, use_global_device_ids=true | all-gather | bytes 9216 | tf_op jit(solution)/shard_map/all_gather | solution.py:19
  477.9 12.9 %all_gather.86 = f32[8,8,32,1]{2,1,3,0:T(8,128)S(1)} all-gather(f32[1,8,32,1]{2,1,3,0:T(8,128)S(1)} %get-tuple-element.1419), channel_id=1, replica_groups=mesh['batch'=8,'tensor'=32] {'batch'}, dimensions={0}, use_global_device_ids=true | all-gather | bytes 9216 | tf_op jit(solution)/shard_map/all_gather | solution.py:19
  490.8 12.9 %all_gather.104 = f32[8,8,32,1]{2,1,3,0:T(8,128)S(1)} all-gather(f32[1,8,32,1]{2,1,3,0:T(8,128)S(1)} %get-tuple-element.1443), channel_id=1, replica_groups=mesh['batch'=8,'tensor'=32] {'batch'}, dimensions={0}, use_global_device_ids=true | all-gather | bytes 9216 | tf_op jit(solution)/shard_map/all_gather | solution.py:19
  503.7 13.1 %all_gather.105 = f32[8,8,32,1]{2,1,3,0:T(8,128)S(1)} all-gather(f32[1,8,32,1]{2,1,3,0:T(8,128)S(1)} %get-tuple-element.1444), channel_id=1, replica_groups=mesh['batch'=8,'tensor'=32] {'batch'}, dimensions={0}, use_global_device_ids=true | all-gather | bytes 9216 | tf_op jit(solution)/shard_map/all_gather | solution.py:19
  516.8 12.9 %all_gather.98 = f32[8,8,32,1]{2,1,3,0:T(8,128)S(1)} all-gather(f32[1,8,32,1]{2,1,3,0:T(8,128)S(1)} %get-tuple-element.1445), channel_id=1, replica_groups=mesh['batch'=8,'tensor'=32] {'batch'}, dimensions={0}, use_global_device_ids=true | all-gather | bytes 9216 | tf_op jit(solution)/shard_map/all_gather | solution.py:19
  529.6 12.9 %all_gather.99 = f32[8,8,32,1]{2,1,3,0:T(8,128)S(1)} all-gather(f32[1,8,32,1]{2,1,3,0:T(8,128)S(1)} %get-tuple-element.1446), channel_id=1, replica_groups=mesh['batch'=8,'tensor'=32] {'batch'}, dimensions={0}, use_global_device_ids=true | all-gather | bytes 9216 | tf_op jit(solution)/shard_map/all_gather | solution.py:19
  542.5 12.9 %all_gather.92 = f32[8,8,32,1]{2,1,3,0:T(8,128)S(1)} all-gather(f32[1,8,32,1]{2,1,3,0:T(8,128)S(1)} %get-tuple-element.1447), channel_id=1, replica_groups=mesh['batch'=8,'tensor'=32] {'batch'}, dimensions={0}, use_global_device_ids=true | all-gather | bytes 9216 | tf_op jit(solution)/shard_map/all_gather | solution.py:19
  555.3 12.9 %all_gather.93 = f32[8,8,32,1]{2,1,3,0:T(8,128)S(1)} all-gather(f32[1,8,32,1]{2,1,3,0:T(8,128)S(1)} %get-tuple-element.1448), channel_id=1, replica_groups=mesh['batch'=8,'tensor'=32] {'batch'}, dimensions={0}, use_global_device_ids=true | all-gather | bytes 9216 | tf_op jit(solution)/shard_map/all_gather | solution.py:19
  568.2 2.8 fusion.50
  571.0 1.6 fusion.17
  573.9 16.4 %while.84 = (s32[]{:T(128)}, f32[8,32,1]{1,2,0:T(1,128)S(1)}, f32[8,32,1]{1,2,0:T(1,128)S(1)}, f32[8,32,1,128]{3,2,1,0:T(1,128)S(1)}, f32[8,8,32,1]{2,1,3,0:T(8,...) while((s32[]{:T(128)}, f32[8,32,1]{1,2,0:T(1,128)S(1)}, ...), condition=%wide.region_7.9_spmd, body=%wide.region_6.8_spmd.sunk | while | flops 99845 | bytes 931983 | solution.py:24
  591.4 11.7 %while.85 = (s32[]{:T(128)}, f32[8,32,1]{1,2,0:T(1,128)S(1)}, f32[8,32,1]{1,2,0:T(1,128)S(1)}, f32[8,32,1,128]{3,2,1,0:T(1,128)S(1)}, f32[8,8,32,1]{2,1,3,0:T(8,...) while((s32[]{:T(128)}, f32[8,32,1]{1,2,0:T(1,128)S(1)}, ...), condition=%wide.region_16.18_spmd, body=%wide.region_15.17_spmd.sunk | while | flops 99845 | bytes 931983 | solution.py:24
  604.3 16.4 %while.87 = (s32[]{:T(128)}, f32[8,32,1]{1,2,0:T(1,128)S(1)}, f32[8,32,1]{1,2,0:T(1,128)S(1)}, f32[8,32,1,128]{3,2,1,0:T(1,128)S(1)}, f32[8,8,32,1]{2,1,3,0:T(8,...) while((s32[]{:T(128)}, f32[8,32,1]{1,2,0:T(1,128)S(1)}, ...), condition=%wide.region_34.36_spmd, body=%wide.region_33.35_spmd.sunk | while | flops 99845 | bytes 931983 | solution.py:24
  624.2 26.7 %while.86 = (s32[]{:T(128)}, f32[8,32,1]{1,2,0:T(1,128)S(1)}, f32[8,32,1]{1,2,0:T(1,128)S(1)}, f32[8,32,1,128]{3,2,1,0:T(1,128)}, f32[8,8,32,1]{2,1,3,0:T(8,128)...) while((s32[]{:T(128)}, f32[8,32,1]{1,2,0:T(1,128)S(1)}, ...), condition=%wide.region_25.27_spmd, body=%wide.region_24.26_spmd.sunk | while | flops 99845 | bytes 931983 | solution.py:24
  625.9 2.2 multiply_add_fusion.21
  629.7 2.2 multiply_add_fusion.21
  633.5 2.2 multiply_add_fusion.21
  637.3 2.2 multiply_add_fusion.21
  641.1 2.2 multiply_add_fusion.21
  644.9 2.2 multiply_add_fusion.21
  648.8 2.2 multiply_add_fusion.21
  650.9 2.3 fusion
  653.2 2.2 fusion.1
  656.6 1.9 fusion.2
  659.1 151.5 %all-reduce.9.cloned.1.call-done = (f32[32,1,4096]{2,0,1:T(8,128)}, f32[32,1,4096]{2,0,1:T(8,128)}, f32[32,1,4096]{2,0,1:T(8,128)}, f32[32,1,4096]{2,0,1:T(8,128)}) async-done(((f32[32,1,4096]{2,0,1:T(8,128)}, f32[32,1,4096]{2,0,1:T(8,128)}, f32[32,1,4096]{2,0,1:T(8,128)}, f32[32,1,4096]{2,0,1:T(8,128)}), (f32[32,1,4096]{2,0,1:T(8,128)}, f32[32,1,4096]{2,0,1:T(8,128)}, f32[32,1,4096]{2,0,1:T(8,128)}, ...) | async-done | bytes 2097168
  810.6 1.8 fusion.208
  (533 shorter events, 188.8 us)
Async XLA Ops:
  6.5 421.4 %copy-start = (bf16[256,4096]{1,0:T(8,128)(2,1)S(1)}, bf16[256,4096]{1,0:T(8,128)(2,1)}, u32[]{:S(2)}) copy-start(bf16[256,4096]{1,0:T(8,128)(2,1)} %param.47) | copy-start | bytes 6291460
  6.5 389.8 %all-gather.14.cloned.1.call-start = ((), (), s32[]{:S(2)}) async-start(), calls=%async_computation | async-start | bytes 9437184 | tf_op jit(solution)/shard_map/all_gather | solution.py:126
  7.3 565.5 %all-gather.16.cloned.1.call-start = ((), (), s32[]{:S(2)}) async-start(), calls=%async_computation.1 | async-start | bytes 1179648 | tf_op jit(solution)/shard_map/all_gather | solution.py:19
  119.0 110.6 %copy-start.4 = (bf16[32,4096]{1,0:T(8,128)(2,1)}, bf16[32,4096]{1,0:T(8,128)(2,1)S(1)}, u32[]{:S(2)}) copy-start(bf16[32,4096]{1,0:T(8,128)(2,1)S(1)} %reshape.3902) | copy-start | bytes 786436
  222.9 9.5 %copy-start.31 = (f32[1,32,384]{2,1,0:T(8,128)}, f32[1,32,384]{2,1,0:T(8,128)S(1)}, u32[]{:S(2)}) copy-start(f32[1,32,384]{2,1,0:T(8,128)S(1)} %convolution_bitcast_fusion.12) | copy-start | bytes 147460
  233.3 7.5 copy-start.48
  234.6 86.4 %copy-start.3 = (bf16[1,32,2,64,128]{4,3,2,1,0:T(8,128)(2,1)S(1)}, bf16[1,32,2,64,128]{4,3,2,1,0:T(8,128)(2,1)}, u32[]{:S(2)}) copy-start(bf16[1,32,2,64,128]{4,3,2,1,0:T(8,128)(2,1)} %param.50) | copy-start | bytes 3145732
  242.6 35.4 %copy-start.11 = (bf16[1,32,64,2]{1,3,2,0:T(2,128)(2,1)}, bf16[1,32,64,2]{1,3,2,0:T(2,128)(2,1)S(1)}, u32[]{:S(2)}) copy-start(bf16[1,32,64,2]{1,3,2,0:T(2,128)(2,1)S(1)} %copy.1412) | copy-start | bytes 24580
  242.8 35.2 %copy-start.13 = (bf16[1,32,64,2]{1,3,2,0:T(2,128)(2,1)}, bf16[1,32,64,2]{1,3,2,0:T(2,128)(2,1)S(1)}, u32[]{:S(2)}) copy-start(bf16[1,32,64,2]{1,3,2,0:T(2,128)(2,1)S(1)} %copy.1439) | copy-start | bytes 24580
  243.6 32.9 %copy-start.15 = (bf16[1,32,64,2]{1,3,2,0:T(2,128)(2,1)}, bf16[1,32,64,2]{1,3,2,0:T(2,128)(2,1)S(1)}, u32[]{:S(2)}) copy-start(bf16[1,32,64,2]{1,3,2,0:T(2,128)(2,1)S(1)} %copy.1466) | copy-start | bytes 24580
  270.6 75.8 %copy-start.68 = (s32[32,4]{0,1:T(4,128)S(1)}, s32[32,4]{0,1:T(4,128)}, u32[]{:S(2)}) copy-start(s32[32,4]{0,1:T(4,128)} %param.51) | copy-start | bytes 1540
  307.7 20.2 %copy-start.10 = (f32[8,32,1,1,4]{4,0,1,3,2:T(8,128)S(1)}, f32[8,32,1,1,4]{4,0,1,3,2:T(8,128)}, u32[]{:S(2)}) copy-start(f32[8,32,1,1,4]{4,0,1,3,2:T(8,128)} %convolution_bitcast_fusion.10) | copy-start | bytes 12292
  307.7 39.4 %copy-start.56 = (s32[4,8,32]{2,1,0:T(8,128)S(1)}, s32[4,8,32]{2,1,0:T(8,128)}, u32[]{:S(2)}) copy-start(s32[4,8,32]{2,1,0:T(8,128)} %param.53) | copy-start | bytes 12292
  322.2 64.8 %collective-permute-start.7 = (f32[8,32,1,1,68]{4,0,1,3,2:T(8,128)}, f32[8,32,1,1,68]{4,0,1,3,2:T(8,128)}, u32[]{:S(2)}, u32[]{:S(2)}) collective-permute-start(f32[8,32,1,1,68]{4,0,1,3,2:T(8,128)} %maximum_multiply_fusion.3), channel_id=1, source_target_pairs={{0,1},{1,0},{2,3},{3,2},{4,5},{5,4},{6,7},{7,6},{8,9},{9,8},{10,11... | collective-permute-start | bytes 208904 | tf_op jit(solution)/shard_map/ppermute | solution.py:15
  325.5 63.4 %collective-permute-start.5 = (f32[8,32,1,1,68]{4,0,1,3,2:T(8,128)}, f32[8,32,1,1,68]{4,0,1,3,2:T(8,128)}, u32[]{:S(2)}, u32[]{:S(2)}) collective-permute-start(f32[8,32,1,1,68]{4,0,1,3,2:T(8,128)} %maximum_multiply_fusion.2), channel_id=1, source_target_pairs={{0,1},{1,0},{2,3},{3,2},{4,5},{5,4},{6,7},{7,6},{8,9},{9,8},{10,11... | collective-permute-start | bytes 208904 | tf_op jit(solution)/shard_map/ppermute | solution.py:15
  328.6 91.0 %collective-permute-start.3 = (f32[8,32,1,1,68]{4,0,1,3,2:T(8,128)}, f32[8,32,1,1,68]{4,0,1,3,2:T(8,128)}, u32[]{:S(2)}, u32[]{:S(2)}) collective-permute-start(f32[8,32,1,1,68]{4,0,1,3,2:T(8,128)} %maximum_multiply_fusion.1), channel_id=1, source_target_pairs={{0,1},{1,0},{2,3},{3,2},{4,5},{5,4},{6,7},{7,6},{8,9},{9,8},{10,11... | collective-permute-start | bytes 208904 | tf_op jit(solution)/shard_map/ppermute | solution.py:15
  329.5 20.5 %copy-start.17 = (bf16[1,32,64,2]{1,3,2,0:T(2,128)(2,1)}, bf16[1,32,64,2]{1,3,2,0:T(2,128)(2,1)S(1)}, u32[]{:S(2)}) copy-start(bf16[1,32,64,2]{1,3,2,0:T(2,128)(2,1)S(1)} %copy.1383) | copy-start | bytes 24580
  343.6 47.2 %collective-permute-start.1 = (f32[8,32,1,1,68]{4,0,1,3,2:T(8,128)}, f32[8,32,1,1,68]{4,0,1,3,2:T(8,128)}, u32[]{:S(2)}, u32[]{:S(2)}) collective-permute-start(f32[8,32,1,1,68]{4,0,1,3,2:T(8,128)} %maximum_multiply_fusion), channel_id=1, source_target_pairs={{0,1},{1,0},{2,3},{3,2},{4,5},{5,4},{6,7},{7,6},{8,9},{9,8},{10,11... | collective-permute-start | bytes 208904 | tf_op jit(solution)/shard_map/ppermute | solution.py:15
  362.5 16.7 %copy-start.12 = (bf16[1,32,64,2]{1,3,2,0:T(2,128)(2,1)S(1)}, bf16[1,32,64,2]{1,3,2,0:T(2,128)(2,1)}, u32[]{:S(2)}) copy-start(bf16[1,32,64,2]{1,3,2,0:T(2,128)(2,1)} %copy-done.11) | copy-start | bytes 24580
  362.5 17.4 %copy-start.14 = (bf16[1,32,64,2]{1,3,2,0:T(2,128)(2,1)S(1)}, bf16[1,32,64,2]{1,3,2,0:T(2,128)(2,1)}, u32[]{:S(2)}) copy-start(bf16[1,32,64,2]{1,3,2,0:T(2,128)(2,1)} %copy-done.13) | copy-start | bytes 24580
  362.5 18.1 %copy-start.16 = (bf16[1,32,64,2]{1,3,2,0:T(2,128)(2,1)S(1)}, bf16[1,32,64,2]{1,3,2,0:T(2,128)(2,1)}, u32[]{:S(2)}) copy-start(bf16[1,32,64,2]{1,3,2,0:T(2,128)(2,1)} %copy-done.15) | copy-start | bytes 24580
  383.5 8.1 copy-start.18
  384.5 9.2 %copy-start.22 = (pred[8,32,1,4]{3,0,1,2:T(8,128)(4,1)}, pred[8,32,1,4]{3,0,1,2:T(8,128)(4,1)S(1)}, u32[]{:S(2)}) copy-start(pred[8,32,1,4]{3,0,1,2:T(8,128)(4,1)S(1)} %compare_bitcast_fusion) | copy-start | bytes 3076
  385.4 7.4 copy-start.21
  386.4 33.4 %copy-start.20 = (pred[8,32,1,4]{3,0,1,2:T(8,128)(4,1)}, pred[8,32,1,4]{3,0,1,2:T(8,128)(4,1)S(1)}, u32[]{:S(2)}) copy-start(pred[8,32,1,4]{3,0,1,2:T(8,128)(4,1)S(1)} %compare_bitcast_fusion.2) | copy-start | bytes 3076
  410.4 15.2 %copy-start.1 = (bf16[32,4,1,128,128]{4,3,2,1,0:T(8,128)(2,1)}, bf16[32,4,1,128,128]{4,3,2,1,0:T(8,128)(2,1)S(1)}, u32[]{:S(2)}) copy-start(bf16[32,4,1,128,128]{4,3,2,1,0:T(8,128)(2,1)S(1)} %get-tuple-element.1348) | copy-start | bytes 12582916
  414.0 5.6 copy-start.49
  414.0 9.8 %copy-start.64 = (s32[32]{0:T(128)S(1)}, s32[32]{0:T(128)}, u32[]{:S(2)}) copy-start(s32[32]{0:T(128)} %param.52) | copy-start | bytes 388
  415.2 11.0 %copy-start.65 = (pred[8]{0:T(512)(128)(4,1)S(1)}, pred[8]{0:T(512)(128)(4,1)}, u32[]{:S(2)}) copy-start(pred[8]{0:T(512)(128)(4,1)} %iota_compare_fusion.2) | copy-start | bytes 28
  415.3 11.7 %copy-start.30 = (bf16[8,32,1,1,68]{4,0,1,3,2:T(8,128)(2,1)S(1)}, bf16[8,32,1,1,68]{4,0,1,3,2:T(8,128)(2,1)}, u32[]{:S(2)}) copy-start(bf16[8,32,1,1,68]{4,0,1,3,2:T(8,128)(2,1)} %copy-done.29) | copy-start | bytes 104452
  415.3 11.7 %copy-start.39 = (f32[32,128,8]{1,2,0:T(8,128)S(1)}, f32[32,128,8]{1,2,0:T(8,128)}, u32[]{:S(2)}) copy-start(f32[32,128,8]{1,2,0:T(8,128)} %fusion.43) | copy-start | bytes 393220
  415.3 5.6 collective-permute-start.6
  415.6 6.4 collective-permute-start.4
  417.6 5.5 collective-permute-start.2
  417.7 6.1 collective-permute-start
  419.7 6.5 copy-start.26
  424.1 7.7 copy-start.59
  427.9 162.4 %all-gather.18.cloned.1.call-start = ((), (), s32[]{:S(2)}) async-start(), calls=%async_computation.2 | async-start | bytes 1179648 | tf_op jit(solution)/shard_map/all_gather | solution.py:19
  435.6 5.1 copy-start.55
  435.6 5.1 copy-start.66
  435.6 6.9 copy-start.51
  437.6 7.7 copy-start.50
  441.7 161.5 %all-gather.22.cloned.1.call-start = ((), (), s32[]{:S(2)}) async-start(), calls=%async_computation.4 | async-start | bytes 1179648 | tf_op jit(solution)/shard_map/all_gather | solution.py:19
  441.7 7.9 copy-start.52
  441.7 7.9 copy-start.53
  451.2 171.3 %all-gather.20.cloned.1.call-start = ((), (), s32[]{:S(2)}) async-start(), calls=%async_computation.3 | async-start | bytes 1179648 | tf_op jit(solution)/shard_map/all_gather | solution.py:19
  455.0 7.9 copy-start.19
  458.9 112.1 %copy-start.28 = (bf16[8,32,1,1,68]{4,0,1,3,2:T(8,128)(2,1)S(1)}, bf16[8,32,1,1,68]{4,0,1,3,2:T(8,128)(2,1)}, u32[]{:S(2)}) copy-start(bf16[8,32,1,1,68]{4,0,1,3,2:T(8,128)(2,1)} %copy-done.27) | copy-start | bytes 104452
  458.9 112.1 %copy-start.38 = (f32[32,128,8]{1,2,0:T(8,128)S(1)}, f32[32,128,8]{1,2,0:T(8,128)}, u32[]{:S(2)}) copy-start(f32[32,128,8]{1,2,0:T(8,128)} %fusion.41) | copy-start | bytes 393220
  477.9 12.9 %copy-start.42 = (f32[8,8,32,1]{2,1,3,0:T(8,128)}, f32[8,8,32,1]{2,1,3,0:T(8,128)S(1)}, u32[]{:S(2)}) copy-start(f32[8,8,32,1]{2,1,3,0:T(8,128)S(1)} %all_gather.87) | copy-start | bytes 24580
  490.8 12.9 %copy-start.43 = (f32[8,8,32,1]{2,1,3,0:T(8,128)}, f32[8,8,32,1]{2,1,3,0:T(8,128)S(1)}, u32[]{:S(2)}) copy-start(f32[8,8,32,1]{2,1,3,0:T(8,128)S(1)} %all_gather.86) | copy-start | bytes 24580
  503.7 13.1 %copy-start.40 = (f32[8,8,32,1]{2,1,3,0:T(8,128)}, f32[8,8,32,1]{2,1,3,0:T(8,128)S(1)}, u32[]{:S(2)}) copy-start(f32[8,8,32,1]{2,1,3,0:T(8,128)S(1)} %all_gather.104) | copy-start | bytes 24580
  516.7 12.9 %copy-start.41 = (f32[8,8,32,1]{2,1,3,0:T(8,128)}, f32[8,8,32,1]{2,1,3,0:T(8,128)S(1)}, u32[]{:S(2)}) copy-start(f32[8,8,32,1]{2,1,3,0:T(8,128)S(1)} %all_gather.105) | copy-start | bytes 24580
  529.6 43.2 %copy-start.35 = (f32[8,8,32,1]{2,1,3,0:T(8,128)}, f32[8,8,32,1]{2,1,3,0:T(8,128)S(1)}, u32[]{:S(2)}) copy-start(f32[8,8,32,1]{2,1,3,0:T(8,128)S(1)} %all_gather.98) | copy-start | bytes 24580
  542.5 30.3 %copy-start.36 = (f32[8,8,32,1]{2,1,3,0:T(8,128)}, f32[8,8,32,1]{2,1,3,0:T(8,128)S(1)}, u32[]{:S(2)}) copy-start(f32[8,8,32,1]{2,1,3,0:T(8,128)S(1)} %all_gather.99) | copy-start | bytes 24580
  572.7 237.9 %all-reduce.9.cloned.1.call-start = ((), (), s32[]{:S(2)}) async-start(), calls=%async_computation.5 | async-start | bytes 4194304
  590.3 14.0 %copy-start.37 = (f32[8,32,1]{1,2,0:T(1,128)}, f32[8,32,1]{1,2,0:T(1,128)S(1)}, u32[]{:S(2)}) copy-start(f32[8,32,1]{1,2,0:T(1,128)S(1)} %get-tuple-element.811) | copy-start | bytes 3076
  603.1 21.0 %slice-start = ((f32[8,8,32,1]{2,1,3,0:T(8,128)}), f32[1,8,32,1]{2,1,3,0:T(8,128)S(1)}, s32[]{:S(2)}) async-start(f32[8,8,32,1]{2,1,3,0:T(8,128)} %copy-done.35), calls=%async_computation.6 | async-start | bytes 8192 | tf_op jit(solution)/shard_map/jit(dynamic_index_in_dim)/dynamic_slice | solution.py:22
  603.2 21.0 %slice-start.1 = ((f32[8,8,32,1]{2,1,3,0:T(8,128)}), f32[1,8,32,1]{2,1,3,0:T(8,128)S(1)}, s32[]{:S(2)}) async-start(f32[8,8,32,1]{2,1,3,0:T(8,128)} %copy-done.36), calls=%async_computation.7 | async-start | bytes 8192 | tf_op jit(solution)/shard_map/jit(dynamic_index_in_dim)/dynamic_slice | solution.py:22
  620.7 30.2 %copy-start.2 = (bf16[128,4096]{1,0:T(8,128)(2,1)S(1)}, bf16[128,4096]{1,0:T(8,128)(2,1)}, u32[]{:S(2)}) copy-start(bf16[128,4096]{1,0:T(8,128)(2,1)} %param.44) | copy-start | bytes 3145732
  624.2 29.0 %copy-start.69 = (f32[32]{0:T(128)S(1)}, f32[32]{0:T(128)}, u32[]{:S(2)}) copy-start(f32[32]{0:T(128)} %fusion.263) | copy-start | bytes 388
  650.9 5.7 copy-start.8
  655.4 155.2 %copy-start.6 = (bf16[4,1,1,4096]{3,0,2,1:T(4,128)(2,1)S(1)}, bf16[4,1,1,4096]{3,0,2,1:T(4,128)(2,1)}, u32[]{:S(2)}) copy-start(bf16[4,1,1,4096]{3,0,2,1:T(4,128)(2,1)} %param.40) | copy-start | bytes 98308
  655.4 155.2 %copy-start.57 = (f32[4096]{0:T(1024)S(1)}, f32[4096]{0:T(1024)}, u32[]{:S(2)}) copy-start(f32[4096]{0:T(1024)} %param.48) | copy-start | bytes 49156
  (23 other events, 53.4 us)
Sparse Core Ops, SparseCore 0:
  9.2 54.3 all-gather.13
  428.0 22.2 all-gather.15
  452.1 26.7 all-gather.17
  480.7 26.8 all-gather.21
  572.8 22.2 all-gather.19
  658.6 151.9 all-reduce.8
where the time goes:
time: 834 us; the launch traced here: 820 us
  blocking collectives  351 us (42%)
  waiting for transfers between devices  155 us (19%)
  local copies, waits for them, and re-layouts  150 us (18%)
  other arithmetic  73.5 us (9%)
  matrix products  59.8 us (7%)
  between operations  20.3 us (2%)
  starting transfers between devices  9 us (1%)
    all_gather x4, blocking collectives, on_device(): gathered_rows = lax.all_gather(normed, 'tensor', axis=1, tiled=True)  196 us
    unnamed x7, waiting for transfers between devices  152 us
    all_gather x8, blocking collectives, joined_2(): gathered = jax.tree.map(lambda a: lax.all_gather(a, axis), part)  103 us
    all_gather x4, blocking collectives, on_device(): queries_all = lax.all_gather(queries, 'batch', axis=0, tiled=True)  51.7 us
    dynamic_slice x98, local copies, waits for them, and re-layouts, take(): lax.dynamic_index_in_dim(a, source, 0, False)  44.8 us
    add x28, other arithmetic, combine(): mixture_one * factor_one[..., None] + mixture_two * factor_two[..., None]  29.2 us
    unnamed x160, local copies, waits for them, and re-layouts  21.6 us
  transfers between devices with their start and end apart: 14, of which 4 were waited for; matrix products, arithmetic and copies ran while one was open for 29% of the time, Pallas kernels for 0%

commit v1 on v0

--- a/solution.py
+++ b/solution.py
@@ -132,7 +132,9 @@
     for step_index in range(STEPS):
         current = inputs[step_index]
         normed = normalize(current, norm_gain, norm_bias).astype(jnp.bfloat16)
-        gathered_rows = lax.all_gather(normed, "tensor", axis=1, tiled=True)
+        gathered_rows = jnp.concatenate(
+            lax.all_to_all(jnp.stack([normed] * lax.axis_size("tensor"), axis=0), "tensor", 0, 0), 1
+        )
         attn_part = jnp.einsum(
             "brd,dc->brc", gathered_rows, qkv_flat, preferred_element_type=jnp.float32
         )

time: 834 us -> 663 us (0.79)
  blocking collectives: 351 us -> 154 us
  starting transfers between devices: 9 us -> 40.7 us
  waiting for transfers between devices: 155 us -> 172 us
  local copies, waits for them, and re-layouts: 150 us -> 135 us
    all_gather x4 -> x0, blocking collectives: 196 us -> none  [on_device(): gathered_rows = lax.all_gather(normed, 'tensor', axis=1, tiled=True)]
    all_to_all x0 -> x4, starting transfers between devices: none -> 31.2 us  [on_device(): lax.all_to_all(jnp.stack([normed] * lax.axis_size('tensor'), axis=0), 'te...]
    all_to_all x0 -> x4, waiting for transfers between devices: none -> 15.5 us  [on_device(): lax.all_to_all(jnp.stack([normed] * lax.axis_size('tensor'), axis=0), 'te...]
    unnamed x160 -> x168, local copies, waits for them, and re-layouts: 21.6 us -> 21.6 us
    dynamic_slice x98 -> x97, local copies, waits for them, and re-layouts: 44.8 us -> 44.7 us  [take(): lax.dynamic_index_in_dim(a, source, 0, False)]
  transfers between devices with their start and end apart: 14 -> 18, of which waited for: 4 -> 7; matrix products, arithmetic and copies ran while one was open for 29% -> 34% of each run, Pallas kernels for 0% -> 0%
where the time goes in v1:
time: 663 us; the launch traced here: 655 us
  waiting for transfers between devices  172 us (26%)
  blocking collectives  154 us (23%)
  local copies, waits for them, and re-layouts  135 us (20%)
  other arithmetic  71.6 us (11%)
  matrix products  60.2 us (9%)
  starting transfers between devices  40.7 us (6%)
  between operations  20.6 us (3%)
    unnamed x7, waiting for transfers between devices  153 us
    all_gather x8, blocking collectives, joined_2(): gathered = jax.tree.map(lambda a: lax.all_gather(a, axis), part)  103 us
    all_gather x4, blocking collectives, on_device(): queries_all = lax.all_gather(queries, 'batch', axis=0, tiled=True)  51.3 us
    dynamic_slice x97, local copies, waits for them, and re-layouts, take(): lax.dynamic_index_in_dim(a, source, 0, False)  44.7 us
    all_to_all x4, starting transfers between devices, on_device(): lax.all_to_all(jnp.stack([normed] * lax.axis_size('tensor'), axis=0), 'te...  31.2 us
    add x28, other arithmetic, combine(): mixture_one * factor_one[..., None] + mixture_two * factor_two[..., None]  29.2 us
    unnamed x168, local copies, waits for them, and re-layouts  21.6 us
    gather x27, local copies, waits for them, and re-layouts, on_device(): lineage = jnp.take_along_axis(parents[back_step], lineage, axis=0)  15.6 us
  transfers between devices with their start and end apart: 18, of which 7 were waited for; matrix products, arithmetic and copies ran while one was open for 34% of the time, Pallas kernels for 0%

profile of v1, /device:TPU:2, one launch (start us, length us, event | category | flops | bytes accessed | tf_op | source)
XLA Modules:
  0.0 655.2 jit_solution(6688143017323564908)
XLA Ops:
  7.3 1.7 convert_reduce_fusion.1
  11.5 1.7 fusion.254
  18.7 2.2 reduce.44
  21.8 11.7 %all-to-all-start.3 = ((bf16[32,2,2048]{2,1,0:T(2,128)(2,1)}), bf16[32,2,2048]{2,1,0:T(2,128)(2,1)S(1)}, u32[]{:S(2)}, u32[]{:S(2)}) async-start(bf16[32,2,2048]{2,1,0:T(2,128)(2,1)} %reshape.4169), calls=%async_computation.3 | async-start | bytes 524288 | tf_op jit(solution)/shard_map/all_to_all | solution.py:136
  39.9 1.4 gather_fusion.8
  41.5 1.4 gather_fusion.5
  43.1 1.4 gather_fusion.3
  59.6 2.2 reduce.46
  63.1 2.2 reduce.45
  66.6 2.2 reduce.47
  69.7 4.8 copy.1379
  75.7 9.9 %all-to-all-start.2 = ((bf16[32,2,2048]{2,1,0:T(2,128)(2,1)}), bf16[32,2,2048]{2,1,0:T(2,128)(2,1)S(1)}, u32[]{:S(2)}, u32[]{:S(2)}) async-start(bf16[32,2,2048]{2,1,0:T(2,128)(2,1)} %reshape.4175), calls=%async_computation.2 | async-start | bytes 524288 | tf_op jit(solution)/shard_map/all_to_all | solution.py:136
  86.6 3.1 convolution_bitcast_fusion.12
  89.7 7.8 %all-to-all-done.2 = bf16[32,2,2048]{2,1,0:T(2,128)(2,1)S(1)} async-done(((bf16[32,2,2048]{2,1,0:T(2,128)(2,1)}), bf16[32,2,2048]{2,1,0:T(2,128)(2,1)S(1)}, u32[]{:S(2)}, u32[]{:S(2)}) %all-to-all-start.2) | async-done | bytes 262176 | tf_op jit(solution)/shard_map/all_to_all | solution.py:136
  97.5 4.5 all-to-all-start.1
  102.7 2.2 reshape.4176
  104.8 3.1 convolution_bitcast_fusion.13
  108.7 4.7 all-to-all-done.1
  114.0 5.1 all-to-all-start
  119.2 2.2 reshape.4174
  122.2 2.9 convolution_bitcast_fusion.14
  127.9 3.0 all-to-all-done
  131.8 3.1 convolution_bitcast_fusion.15
  146.5 12.7 %all_gather.77 = bf16[8,32,128]{2,1,0:T(8,128)(2,1)S(1)} all-gather(bf16[1,32,128]{2,1,0:T(8,128)(2,1)S(1)} %copy.1416), channel_id=1, replica_groups=mesh['batch'=8,'tensor'=32] {'batch'}, dimensions={0}, use_global_device_ids=true | all-gather | bytes 73728 | tf_op jit(solution)/shard_map/all_gather | solution.py:158
  160.1 12.8 %all_gather.82 = bf16[8,32,128]{2,1,0:T(8,128)(2,1)S(1)} all-gather(bf16[1,32,128]{2,1,0:T(8,128)(2,1)S(1)} %copy.1443), channel_id=1, replica_groups=mesh['batch'=8,'tensor'=32] {'batch'}, dimensions={0}, use_global_device_ids=true | all-gather | bytes 73728 | tf_op jit(solution)/shard_map/all_gather | solution.py:158
  173.8 12.9 %all_gather.87 = bf16[8,32,128]{2,1,0:T(8,128)(2,1)S(1)} all-gather(bf16[1,32,128]{2,1,0:T(8,128)(2,1)S(1)} %copy.1470), channel_id=1, replica_groups=mesh['batch'=8,'tensor'=32] {'batch'}, dimensions={0}, use_global_device_ids=true | all-gather | bytes 73728 | tf_op jit(solution)/shard_map/all_gather | solution.py:158
  192.8 12.9 %all_gather.72 = bf16[8,32,128]{2,1,0:T(8,128)(2,1)S(1)} all-gather(bf16[1,32,128]{2,1,0:T(8,128)(2,1)} %copy.1387), channel_id=1, replica_groups=mesh['batch'=8,'tensor'=32] {'batch'}, dimensions={0}, use_global_device_ids=true | all-gather | bytes 73728 | tf_op jit(solution)/shard_map/all_gather | solution.py:158
  209.2 1.6 fusion.47
  211.5 1.6 fusion.46
  216.7 10.1 %gather_fusion = bf16[128,2,128,128]{3,2,1,0:T(8,128)(2,1)} fusion(bf16[128,2,128,128]{3,2,1,0:T(8,128)(2,1)} %all-gather.10.cloned.1.call-done, s32[1024]{0:T(1024)} %pad_clamp_fusion), kind=kCustom, calls=%fused_computation.10 | custom fusion | bytes 16777728 | tf_op jit(solution)/shard_map/gather | solution.py:127
  226.8 4.0 fusion.327
  248.6 3.8 fusion.131
  252.4 3.8 fusion.116
  260.4 2.8 fusion.68
  268.2 1.6 fusion.57
  274.0 2.8 fusion.64
  277.9 3.8 fusion.101
  281.6 3.8 fusion.146
  290.2 1.8 select_reduce_fusion
  297.4 12.9 %all_gather.74 = f32[8,8,32,1]{2,1,3,0:T(8,128)S(1)} all-gather(f32[1,8,32,1]{2,1,3,0:T(8,128)S(1)} %get-tuple-element.1418), channel_id=1, replica_groups=mesh['batch'=8,'tensor'=32] {'batch'}, dimensions={0}, use_global_device_ids=true | all-gather | bytes 9216 | tf_op jit(solution)/shard_map/all_gather | solution.py:19
  310.3 12.9 %all_gather.73 = f32[8,8,32,1]{2,1,3,0:T(8,128)S(1)} all-gather(f32[1,8,32,1]{2,1,3,0:T(8,128)S(1)} %get-tuple-element.1419), channel_id=1, replica_groups=mesh['batch'=8,'tensor'=32] {'batch'}, dimensions={0}, use_global_device_ids=true | all-gather | bytes 9216 | tf_op jit(solution)/shard_map/all_gather | solution.py:19
  323.8 12.9 %all_gather.88 = f32[8,8,32,1]{2,1,3,0:T(8,128)S(1)} all-gather(f32[1,8,32,1]{2,1,3,0:T(8,128)S(1)} %get-tuple-element.1443), channel_id=1, replica_groups=mesh['batch'=8,'tensor'=32] {'batch'}, dimensions={0}, use_global_device_ids=true | all-gather | bytes 9216 | tf_op jit(solution)/shard_map/all_gather | solution.py:19
  336.7 12.9 %all_gather.89 = f32[8,8,32,1]{2,1,3,0:T(8,128)S(1)} all-gather(f32[1,8,32,1]{2,1,3,0:T(8,128)S(1)} %get-tuple-element.1444), channel_id=1, replica_groups=mesh['batch'=8,'tensor'=32] {'batch'}, dimensions={0}, use_global_device_ids=true | all-gather | bytes 9216 | tf_op jit(solution)/shard_map/all_gather | solution.py:19
  349.5 12.9 %all_gather.83 = f32[8,8,32,1]{2,1,3,0:T(8,128)S(1)} all-gather(f32[1,8,32,1]{2,1,3,0:T(8,128)S(1)} %get-tuple-element.1445), channel_id=1, replica_groups=mesh['batch'=8,'tensor'=32] {'batch'}, dimensions={0}, use_global_device_ids=true | all-gather | bytes 9216 | tf_op jit(solution)/shard_map/all_gather | solution.py:19
  363.0 12.9 %all_gather.84 = f32[8,8,32,1]{2,1,3,0:T(8,128)S(1)} all-gather(f32[1,8,32,1]{2,1,3,0:T(8,128)S(1)} %get-tuple-element.1446), channel_id=1, replica_groups=mesh['batch'=8,'tensor'=32] {'batch'}, dimensions={0}, use_global_device_ids=true | all-gather | bytes 9216 | tf_op jit(solution)/shard_map/all_gather | solution.py:19
  375.8 12.9 %all_gather.78 = f32[8,8,32,1]{2,1,3,0:T(8,128)S(1)} all-gather(f32[1,8,32,1]{2,1,3,0:T(8,128)S(1)} %get-tuple-element.1447), channel_id=1, replica_groups=mesh['batch'=8,'tensor'=32] {'batch'}, dimensions={0}, use_global_device_ids=true | all-gather | bytes 9216 | tf_op jit(solution)/shard_map/all_gather | solution.py:19
  388.7 12.9 %all_gather.79 = f32[8,8,32,1]{2,1,3,0:T(8,128)S(1)} all-gather(f32[1,8,32,1]{2,1,3,0:T(8,128)S(1)} %get-tuple-element.1448), channel_id=1, replica_groups=mesh['batch'=8,'tensor'=32] {'batch'}, dimensions={0}, use_global_device_ids=true | all-gather | bytes 9216 | tf_op jit(solution)/shard_map/all_gather | solution.py:19
  401.6 2.8 fusion.66
  406.7 16.4 %while.84 = (s32[]{:T(128)}, f32[8,32,1]{1,2,0:T(1,128)S(1)}, f32[8,32,1]{1,2,0:T(1,128)S(1)}, f32[8,32,1,128]{3,2,1,0:T(1,128)S(1)}, f32[8,8,32,1]{2,1,3,0:T(8,...) while((s32[]{:T(128)}, f32[8,32,1]{1,2,0:T(1,128)S(1)}, ...), condition=%wide.region_7.9_spmd, body=%wide.region_6.8_spmd.sunk | while | flops 99845 | bytes 931983 | solution.py:24
  424.2 11.7 %while.85 = (s32[]{:T(128)}, f32[8,32,1]{1,2,0:T(1,128)S(1)}, f32[8,32,1]{1,2,0:T(1,128)S(1)}, f32[8,32,1,128]{3,2,1,0:T(1,128)S(1)}, f32[8,8,32,1]{2,1,3,0:T(8,...) while((s32[]{:T(128)}, f32[8,32,1]{1,2,0:T(1,128)S(1)}, ...), condition=%wide.region_16.18_spmd, body=%wide.region_15.17_spmd.sunk | while | flops 99845 | bytes 931983 | solution.py:24
  437.6 16.4 %while.87 = (s32[]{:T(128)}, f32[8,32,1]{1,2,0:T(1,128)S(1)}, f32[8,32,1]{1,2,0:T(1,128)S(1)}, f32[8,32,1,128]{3,2,1,0:T(1,128)S(1)}, f32[8,8,32,1]{2,1,3,0:T(8,...) while((s32[]{:T(128)}, f32[8,32,1]{1,2,0:T(1,128)S(1)}, ...), condition=%wide.region_34.36_spmd, body=%wide.region_33.35_spmd.sunk | while | flops 99845 | bytes 931983 | solution.py:24
  458.2 26.7 %while.86 = (s32[]{:T(128)}, f32[8,32,1]{1,2,0:T(1,128)S(1)}, f32[8,32,1]{1,2,0:T(1,128)S(1)}, f32[8,32,1,128]{3,2,1,0:T(1,128)}, f32[8,8,32,1]{2,1,3,0:T(8,128)...) while((s32[]{:T(128)}, f32[8,32,1]{1,2,0:T(1,128)S(1)}, ...), condition=%wide.region_25.27_spmd, body=%wide.region_24.26_spmd.sunk | while | flops 99845 | bytes 931983 | solution.py:24
  459.9 2.2 multiply_add_fusion.21
  463.7 2.2 multiply_add_fusion.21
  467.5 2.2 multiply_add_fusion.21
  471.4 2.2 multiply_add_fusion.21
  475.2 2.2 multiply_add_fusion.21
  479.0 2.2 multiply_add_fusion.21
  482.8 2.2 multiply_add_fusion.21
  485.0 2.2 fusion
  487.2 2.2 fusion.1
  490.6 1.9 fusion.2
  493.1 152.5 %all-reduce.9.cloned.1.call-done = (f32[32,1,4096]{2,0,1:T(8,128)}, f32[32,1,4096]{2,0,1:T(8,128)}, f32[32,1,4096]{2,0,1:T(8,128)}, f32[32,1,4096]{2,0,1:T(8,128)}) async-done(((f32[32,1,4096]{2,0,1:T(8,128)}, f32[32,1,4096]{2,0,1:T(8,128)}, f32[32,1,4096]{2,0,1:T(8,128)}, f32[32,1,4096]{2,0,1:T(8,128)}), (f32[32,1,4096]{2,0,1:T(8,128)}, f32[32,1,4096]{2,0,1:T(8,128)}, f32[32,1,4096]{2,0,1:T(8,128)}, ...) | async-done | bytes 2097168
  645.6 1.8 fusion.248
  (549 shorter events, 175.2 us)
Async XLA Ops:
  6.5 242.0 %copy-start = (bf16[256,4096]{1,0:T(8,128)(2,1)S(1)}, bf16[256,4096]{1,0:T(8,128)(2,1)}, u32[]{:S(2)}) copy-start(bf16[256,4096]{1,0:T(8,128)(2,1)} %param.47) | copy-start | bytes 6291460
  6.5 27.0 %copy-start.68 = (s32[32,4]{0,1:T(4,128)S(1)}, s32[32,4]{0,1:T(4,128)}, u32[]{:S(2)}) copy-start(s32[32,4]{0,1:T(4,128)} %param.51) | copy-start | bytes 1540
  6.5 27.2 %copy-start.56 = (s32[4,8,32]{2,1,0:T(8,128)S(1)}, s32[4,8,32]{2,1,0:T(8,128)}, u32[]{:S(2)}) copy-start(s32[4,8,32]{2,1,0:T(8,128)} %param.53) | copy-start | bytes 12292
  6.5 210.1 %all-gather.10.cloned.1.call-start = ((), (), s32[]{:S(2)}) async-start(), calls=%async_computation.4 | async-start | bytes 9437184 | tf_op jit(solution)/shard_map/all_gather | solution.py:126
  21.8 54.0 %all-to-all-start.3 = ((bf16[32,2,2048]{2,1,0:T(2,128)(2,1)}), bf16[32,2,2048]{2,1,0:T(2,128)(2,1)S(1)}, u32[]{:S(2)}, u32[]{:S(2)}) async-start(bf16[32,2,2048]{2,1,0:T(2,128)(2,1)} %reshape.4169), calls=%async_computation.3 | async-start | bytes 524288 | tf_op jit(solution)/shard_map/all_to_all | solution.py:136
  75.7 21.7 %all-to-all-start.2 = ((bf16[32,2,2048]{2,1,0:T(2,128)(2,1)}), bf16[32,2,2048]{2,1,0:T(2,128)(2,1)S(1)}, u32[]{:S(2)}, u32[]{:S(2)}) async-start(bf16[32,2,2048]{2,1,0:T(2,128)(2,1)} %reshape.4175), calls=%async_computation.2 | async-start | bytes 524288 | tf_op jit(solution)/shard_map/all_to_all | solution.py:136
  86.6 21.4 %copy-start.8 = (bf16[32,1,1,4096]{3,2,1,0:T(2,128)(2,1)}, bf16[32,1,1,4096]{3,2,1,0:T(2,128)(2,1)S(1)}, u32[]{:S(2)}) copy-start(bf16[32,1,1,4096]{3,2,1,0:T(2,128)(2,1)S(1)} %reshape.4170) | copy-start | bytes 786436
  89.7 12.9 %copy-start.30 = (f32[1,32,384]{2,1,0:T(8,128)}, f32[1,32,384]{2,1,0:T(8,128)S(1)}, u32[]{:S(2)}) copy-start(f32[1,32,384]{2,1,0:T(8,128)S(1)} %convolution_bitcast_fusion.12) | copy-start | bytes 147460
  97.5 15.8 %all-to-all-start.1 = ((bf16[32,2,2048]{2,1,0:T(2,128)(2,1)}), bf16[32,2,2048]{2,1,0:T(2,128)(2,1)S(1)}, u32[]{:S(2)}, u32[]{:S(2)}) async-start(bf16[32,2,2048]{2,1,0:T(2,128)(2,1)} %reshape.4173), calls=%async_computation.1 | async-start | bytes 524288 | tf_op jit(solution)/shard_map/all_to_all | solution.py:136
  104.8 20.2 %copy-start.9 = (bf16[32,1,1,4096]{3,2,1,0:T(2,128)(2,1)}, bf16[32,1,1,4096]{3,2,1,0:T(2,128)(2,1)S(1)}, u32[]{:S(2)}) copy-start(bf16[32,1,1,4096]{3,2,1,0:T(2,128)(2,1)S(1)} %reshape.4176) | copy-start | bytes 786436
  114.0 16.9 %all-to-all-start = ((bf16[32,2,2048]{2,1,0:T(2,128)(2,1)}), bf16[32,2,2048]{2,1,0:T(2,128)(2,1)S(1)}, u32[]{:S(2)}, u32[]{:S(2)}) async-start(bf16[32,2,2048]{2,1,0:T(2,128)(2,1)} %reshape.4171), calls=%async_computation | async-start | bytes 524288 | tf_op jit(solution)/shard_map/all_to_all | solution.py:136
  119.2 286.5 %all-gather.12.cloned.1.call-start = ((), (), s32[]{:S(2)}) async-start(), calls=%async_computation.5 | async-start | bytes 1179648 | tf_op jit(solution)/shard_map/all_gather | solution.py:19
  121.4 9.5 %copy-start.10 = (bf16[32,1,1,4096]{3,2,1,0:T(2,128)(2,1)}, bf16[32,1,1,4096]{3,2,1,0:T(2,128)(2,1)S(1)}, u32[]{:S(2)}) copy-start(bf16[32,1,1,4096]{3,2,1,0:T(2,128)(2,1)S(1)} %reshape.4174) | copy-start | bytes 786436
  125.1 16.8 %copy-start.32 = (f32[1,32,384]{2,1,0:T(8,128)}, f32[1,32,384]{2,1,0:T(8,128)S(1)}, u32[]{:S(2)}) copy-start(f32[1,32,384]{2,1,0:T(8,128)S(1)} %convolution_bitcast_fusion.14) | copy-start | bytes 147460
  131.8 55.0 %copy-start.3 = (bf16[1,32,2,64,128]{4,3,2,1,0:T(8,128)(2,1)S(1)}, bf16[1,32,2,64,128]{4,3,2,1,0:T(8,128)(2,1)}, u32[]{:S(2)}) copy-start(bf16[1,32,2,64,128]{4,3,2,1,0:T(8,128)(2,1)} %param.50) | copy-start | bytes 3145732
  173.8 17.6 %copy-start.17 = (f32[8,32,1,1,4]{4,0,1,3,2:T(8,128)S(1)}, f32[8,32,1,1,4]{4,0,1,3,2:T(8,128)}, u32[]{:S(2)}) copy-start(f32[8,32,1,1,4]{4,0,1,3,2:T(8,128)} %convolution_bitcast_fusion.10) | copy-start | bytes 12292
  173.8 41.1 %copy-start.49 = (pred[8,32]{0,1:T(8,128)(4,1)S(1)}, pred[8,32]{0,1:T(8,128)(4,1)}, u32[]{:S(2)}) copy-start(pred[8,32]{0,1:T(8,128)(4,1)} %copy.1384) | copy-start | bytes 772
  173.8 41.2 %copy-start.39 = (pred[8,32,1,1,4]{4,0,1,3,2:T(8,128)(4,1)S(1)}, pred[8,32,1,1,4]{4,0,1,3,2:T(8,128)(4,1)}, u32[]{:S(2)}) copy-start(pred[8,32,1,1,4]{4,0,1,3,2:T(8,128)(4,1)} %copy.1400) | copy-start | bytes 3076
  187.4 21.0 %collective-permute-start.7 = (f32[8,32,1,1,68]{4,0,1,3,2:T(8,128)S(1)}, f32[8,32,1,1,68]{4,0,1,3,2:T(8,128)S(1)}, u32[]{:S(2)}, u32[]{:S(2)}) collective-permute-start(f32[8,32,1,1,68]{4,0,1,3,2:T(8,128)S(1)} %maximum_multiply_fusion.3), channel_id=1, source_target_pairs={{0,1},{1,0},{2,3},{3,2},{4,5},{5,4},{6,7},{7,6},{8,9},{9,8},{10,11... | collective-permute-start | bytes 208904 | tf_op jit(solution)/shard_map/ppermute | solution.py:15
  190.1 20.6 %collective-permute-start.5 = (f32[8,32,1,1,68]{4,0,1,3,2:T(8,128)S(1)}, f32[8,32,1,1,68]{4,0,1,3,2:T(8,128)S(1)}, u32[]{:S(2)}, u32[]{:S(2)}) collective-permute-start(f32[8,32,1,1,68]{4,0,1,3,2:T(8,128)S(1)} %maximum_multiply_fusion.2), channel_id=1, source_target_pairs={{0,1},{1,0},{2,3},{3,2},{4,5},{5,4},{6,7},{7,6},{8,9},{9,8},{10,11... | collective-permute-start | bytes 208904 | tf_op jit(solution)/shard_map/ppermute | solution.py:15
  191.4 48.5 %collective-permute-start.3 = (f32[8,32,1,1,68]{4,0,1,3,2:T(8,128)S(1)}, f32[8,32,1,1,68]{4,0,1,3,2:T(8,128)}, u32[]{:S(2)}, u32[]{:S(2)}) collective-permute-start(f32[8,32,1,1,68]{4,0,1,3,2:T(8,128)S(1)} %maximum_multiply_fusion.1), channel_id=1, source_target_pairs={{0,1},{1,0},{2,3},{3,2},{4,5},{5,4},{6,7},{7,6},{8,9},{9,8},{10,11... | collective-permute-start | bytes 208904 | tf_op jit(solution)/shard_map/ppermute | solution.py:15
  206.4 8.6 %copy-start.4 = (f32[8,32,1,1,68]{4,0,1,3,2:T(8,128)}, f32[8,32,1,1,68]{4,0,1,3,2:T(8,128)S(1)}, u32[]{:S(2)}) copy-start(f32[8,32,1,1,68]{4,0,1,3,2:T(8,128)S(1)} %maximum_multiply_fusion) | copy-start | bytes 208900
  206.4 6.7 %collective-permute-start.1 = (f32[8,32,1,1,68]{4,0,1,3,2:T(8,128)S(1)}, f32[8,32,1,1,68]{4,0,1,3,2:T(8,128)S(1)}, u32[]{:S(2)}, u32[]{:S(2)}) collective-permute-start(f32[8,32,1,1,68]{4,0,1,3,2:T(8,128)S(1)} %maximum_multiply_fusion), channel_id=1, source_target_pairs={{0,1},{1,0},{2,3},{3,2},{4,5},{5,4},{6,7},{7,6},{8,9},{9,8},{10,11... | collective-permute-start | bytes 208904 | tf_op jit(solution)/shard_map/ppermute | solution.py:15
  208.4 6.8 %copy-start.16 = (bf16[32,4,128]{2,0,1:T(8,128)(2,1)}, bf16[32,4,128]{2,0,1:T(8,128)(2,1)S(1)}, u32[]{:S(2)}) copy-start(bf16[32,4,128]{2,0,1:T(8,128)(2,1)S(1)} %pad_bitcast_fusion) | copy-start | bytes 98308
  208.4 6.8 %copy-start.11 = (f32[8,32,1,1,68]{4,0,1,3,2:T(8,128)}, f32[8,32,1,1,68]{4,0,1,3,2:T(8,128)S(1)}, u32[]{:S(2)}) copy-start(f32[8,32,1,1,68]{4,0,1,3,2:T(8,128)S(1)} %collective-permute-done.7) | copy-start | bytes 208900
  230.9 15.2 %copy-start.1 = (bf16[32,4,1,128,128]{4,3,2,1,0:T(8,128)(2,1)}, bf16[32,4,1,128,128]{4,3,2,1,0:T(8,128)(2,1)S(1)}, u32[]{:S(2)}) copy-start(bf16[32,4,1,128,128]{4,3,2,1,0:T(8,128)(2,1)S(1)} %get-tuple-element.1348) | copy-start | bytes 12582916
  234.5 5.6 copy-start.21
  234.5 9.9 %copy-start.63 = (s32[32]{0:T(128)S(1)}, s32[32]{0:T(128)}, u32[]{:S(2)}) copy-start(s32[32]{0:T(128)} %param.52) | copy-start | bytes 388
  235.7 11.0 %copy-start.18 = (f32[8,32]{0,1:T(8,128)S(1)}, f32[8,32]{0,1:T(8,128)}, u32[]{:S(2)}) copy-start(f32[8,32]{0,1:T(8,128)} %fusion.46) | copy-start | bytes 3076
  235.7 11.0 %copy-start.19 = (f32[8,32]{0,1:T(8,128)S(1)}, f32[8,32]{0,1:T(8,128)}, u32[]{:S(2)}) copy-start(f32[8,32]{0,1:T(8,128)} %fusion.47) | copy-start | bytes 3076
  235.7 11.0 %copy-start.64 = (pred[8]{0:T(512)(128)(4,1)S(1)}, pred[8]{0:T(512)(128)(4,1)}, u32[]{:S(2)}) copy-start(pred[8]{0:T(512)(128)(4,1)} %iota_compare_fusion.2) | copy-start | bytes 28
  235.8 11.8 %copy-start.29 = (bf16[8,32,1,1,68]{4,0,1,3,2:T(8,128)(2,1)S(1)}, bf16[8,32,1,1,68]{4,0,1,3,2:T(8,128)(2,1)}, u32[]{:S(2)}) copy-start(bf16[8,32,1,1,68]{4,0,1,3,2:T(8,128)(2,1)} %copy-done.28) | copy-start | bytes 104452
  235.8 11.8 %copy-start.38 = (f32[32,128,8]{1,2,0:T(8,128)S(1)}, f32[32,128,8]{1,2,0:T(8,128)}, u32[]{:S(2)}) copy-start(f32[32,128,8]{1,2,0:T(8,128)} %fusion.59) | copy-start | bytes 393220
  235.8 5.4 collective-permute-start.6
  237.2 5.0 collective-permute-start.4
  237.9 5.7 collective-permute-start.2
  239.2 5.2 collective-permute-start
  240.1 7.4 %copy-start.25 = (pred[8,32,1,64]{3,0,1,2:T(8,128)(4,1)}, pred[8,32,1,64]{3,0,1,2:T(8,128)(4,1)S(1)}, u32[]{:S(2)}) copy-start(pred[8,32,1,64]{3,0,1,2:T(8,128)(4,1)S(1)} %broadcast_in_dim.384) | copy-start | bytes 49156
  241.2 6.3 copy-start.20
  248.5 174.7 %all-gather.14.cloned.1.call-start = ((), (), s32[]{:S(2)}) async-start(), calls=%async_computation.6 | async-start | bytes 1179648 | tf_op jit(solution)/shard_map/all_gather | solution.py:19
  256.2 7.0 %copy-start.54 = (f32[8,32]{0,1:T(8,128)S(1)}, f32[8,32]{0,1:T(8,128)}, u32[]{:S(2)}) copy-start(f32[8,32]{0,1:T(8,128)} %get-tuple-element.1440) | copy-start | bytes 3076
  256.2 7.0 %copy-start.55 = (f32[8,32]{0,1:T(8,128)S(1)}, f32[8,32]{0,1:T(8,128)}, u32[]{:S(2)}) copy-start(f32[8,32]{0,1:T(8,128)} %get-tuple-element.1441) | copy-start | bytes 3076
  256.2 7.0 %copy-start.65 = (pred[8]{0:T(512)(128)(4,1)S(1)}, pred[8]{0:T(512)(128)(4,1)}, u32[]{:S(2)}) copy-start(pred[8]{0:T(512)(128)(4,1)} %iota_compare_fusion.2) | copy-start | bytes 28
  264.2 171.9 %all-gather.18.cloned.1.call-start = ((), (), s32[]{:S(2)}) async-start(), calls=%async_computation.8 | async-start | bytes 1179648 | tf_op jit(solution)/shard_map/all_gather | solution.py:19
  264.4 12.5 %copy-start.52 = (f32[8,32]{0,1:T(8,128)S(1)}, f32[8,32]{0,1:T(8,128)}, u32[]{:S(2)}) copy-start(f32[8,32]{0,1:T(8,128)} %get-tuple-element.1436) | copy-start | bytes 3076
  264.4 12.5 %copy-start.53 = (f32[8,32]{0,1:T(8,128)S(1)}, f32[8,32]{0,1:T(8,128)}, u32[]{:S(2)}) copy-start(f32[8,32]{0,1:T(8,128)} %get-tuple-element.1437) | copy-start | bytes 3076
  264.4 12.5 %copy-start.66 = (pred[8]{0:T(512)(128)(4,1)S(1)}, pred[8]{0:T(512)(128)(4,1)}, u32[]{:S(2)}) copy-start(pred[8]{0:T(512)(128)(4,1)} %iota_compare_fusion.2) | copy-start | bytes 28
  277.8 178.7 %all-gather.16.cloned.1.call-start = ((), (), s32[]{:S(2)}) async-start(), calls=%async_computation.7 | async-start | bytes 1179648 | tf_op jit(solution)/shard_map/all_gather | solution.py:19
  292.0 112.4 %copy-start.27 = (bf16[8,32,1,1,68]{4,0,1,3,2:T(8,128)(2,1)S(1)}, bf16[8,32,1,1,68]{4,0,1,3,2:T(8,128)(2,1)}, u32[]{:S(2)}) copy-start(bf16[8,32,1,1,68]{4,0,1,3,2:T(8,128)(2,1)} %copy-done.26) | copy-start | bytes 104452
  294.0 110.4 %copy-start.37 = (f32[32,128,8]{1,2,0:T(8,128)S(1)}, f32[32,128,8]{1,2,0:T(8,128)}, u32[]{:S(2)}) copy-start(f32[32,128,8]{1,2,0:T(8,128)} %fusion.57) | copy-start | bytes 393220
  296.6 107.8 %copy-start.50 = (f32[8,32]{0,1:T(8,128)S(1)}, f32[8,32]{0,1:T(8,128)}, u32[]{:S(2)}) copy-start(f32[8,32]{0,1:T(8,128)} %get-tuple-element.1438) | copy-start | bytes 3076
  296.6 107.8 %copy-start.51 = (f32[8,32]{0,1:T(8,128)S(1)}, f32[8,32]{0,1:T(8,128)}, u32[]{:S(2)}) copy-start(f32[8,32]{0,1:T(8,128)} %get-tuple-element.1439) | copy-start | bytes 3076
  296.6 107.8 %copy-start.67 = (pred[8]{0:T(512)(128)(4,1)S(1)}, pred[8]{0:T(512)(128)(4,1)}, u32[]{:S(2)}) copy-start(pred[8]{0:T(512)(128)(4,1)} %iota_compare_fusion.2) | copy-start | bytes 28
  336.7 12.9 %copy-start.41 = (f32[8,8,32,1]{2,1,3,0:T(8,128)}, f32[8,8,32,1]{2,1,3,0:T(8,128)S(1)}, u32[]{:S(2)}) copy-start(f32[8,8,32,1]{2,1,3,0:T(8,128)S(1)} %all_gather.88) | copy-start | bytes 24580
  349.5 57.2 %copy-start.42 = (f32[8,8,32,1]{2,1,3,0:T(8,128)}, f32[8,8,32,1]{2,1,3,0:T(8,128)S(1)}, u32[]{:S(2)}) copy-start(f32[8,8,32,1]{2,1,3,0:T(8,128)S(1)} %all_gather.89) | copy-start | bytes 24580
  375.8 29.8 %copy-start.34 = (f32[8,8,32,1]{2,1,3,0:T(8,128)}, f32[8,8,32,1]{2,1,3,0:T(8,128)S(1)}, u32[]{:S(2)}) copy-start(f32[8,8,32,1]{2,1,3,0:T(8,128)S(1)} %all_gather.84) | copy-start | bytes 24580
  405.4 240.2 %all-reduce.9.cloned.1.call-start = ((), (), s32[]{:S(2)}) async-start(), calls=%async_computation.9 | async-start | bytes 4194304
  423.1 12.9 %copy-start.36 = (f32[8,32,1]{1,2,0:T(1,128)}, f32[8,32,1]{1,2,0:T(1,128)S(1)}, u32[]{:S(2)}) copy-start(f32[8,32,1]{1,2,0:T(1,128)S(1)} %get-tuple-element.811) | copy-start | bytes 3076
  436.0 22.2 %slice-start = ((f32[8,8,32,1]{2,1,3,0:T(8,128)}), f32[1,8,32,1]{2,1,3,0:T(8,128)S(1)}, s32[]{:S(2)}) async-start(f32[8,8,32,1]{2,1,3,0:T(8,128)} %copy-done.34), calls=%async_computation.10 | async-start | bytes 8192 | tf_op jit(solution)/shard_map/jit(dynamic_index_in_dim)/dynamic_slice | solution.py:22
  454.0 30.9 %copy-start.2 = (bf16[128,4096]{1,0:T(8,128)(2,1)S(1)}, bf16[128,4096]{1,0:T(8,128)(2,1)}, u32[]{:S(2)}) copy-start(bf16[128,4096]{1,0:T(8,128)(2,1)} %param.44) | copy-start | bytes 3145732
  458.2 29.0 %copy-start.69 = (f32[32]{0:T(128)S(1)}, f32[32]{0:T(128)}, u32[]{:S(2)}) copy-start(f32[32]{0:T(128)} %fusion.303) | copy-start | bytes 388
  485.0 5.6 copy-start.6
  489.4 156.1 %copy-start.5 = (bf16[4,1,1,4096]{3,0,2,1:T(4,128)(2,1)S(1)}, bf16[4,1,1,4096]{3,0,2,1:T(4,128)(2,1)}, u32[]{:S(2)}) copy-start(bf16[4,1,1,4096]{3,0,2,1:T(4,128)(2,1)} %param.40) | copy-start | bytes 98308
  489.4 156.1 %copy-start.57 = (f32[4096]{0:T(1024)S(1)}, f32[4096]{0:T(1024)}, u32[]{:S(2)}) copy-start(f32[4096]{0:T(1024)} %param.48) | copy-start | bytes 49156
  (26 other events, 56.4 us)
Sparse Core Ops, SparseCore 0:
  9.2 54.3 all-gather.9
  248.6 23.0 all-gather.11
  273.6 26.7 all-gather.13
  302.1 26.8 all-gather.17
  405.5 23.1 all-gather.15
  492.6 152.9 all-reduce.8
